TPU v7x, 256 devices: a whole 4x4x8 slice. The times are simulated.
256 devices in a mesh: dp: 32 (over x, z_hi, y), mp: 8 (over z_lo, core).
Axes of the slice: x: 4, y: 4, z: 8 (z_hi: 2, z_lo: 4; z = z_hi * 4 + z_lo), core: 2. Of those that a mesh axis runs over, the one named last changes fastest.
Arguments:
- forget_rows: bfloat16 [1024, 8192], P('dp', 'mp'), may hold values from -6 to 6
- cotangent: bfloat16 [1024, 8192], P('dp', 'mp'), may hold values from -6 to 6
- retain_rows: bfloat16 [1024, 8192], P('dp', 'mp'), may hold values from -6 to 6
- w_gate: bfloat16 [8192, 16384], P('mp', 'dp'), may hold values from -5 to 5
- w_up: bfloat16 [8192, 16384], P('mp', 'dp'), may hold values from -5 to 5
- w_down: bfloat16 [16384, 8192], P('dp', 'mp'), may hold values from -5 to 5
Outputs:
- retained: bfloat16 [1024, 8192], P('dp', 'mp')
- new_gate: bfloat16 [8192, 16384], P('mp', 'dp')
- new_up: bfloat16 [8192, 16384], P('mp', 'dp')
- new_down: bfloat16 [16384, 8192], P('dp', 'mp')
All inputs are finite; a program needn't handle non-finite values.
Results may differ from a plain program's by a relative error of at most 0.0071.
Values may be sent and summed in bfloat16 or wider, within the bound.
No kernel may reach another device: no remote copies, remote signals or barrier semaphores. Data moves between devices by JAX's collectives and lax.ppermute only.
A program may use at most 64 MiB of HBM per device.

v0:
```python
import math
import jax
import jax.numpy as jnp
from jax import lax
from jax.sharding import PartitionSpec as P

D = 8192
FF = 16384
STEP_SIZE = 0.5


def project_sum(rows_all, weight_pair):
    width_scale = 1.0 / math.sqrt(D)
    return lax.psum_scatter(
        jnp.dot(rows_all, weight_pair, preferred_element_type=jnp.float32) * width_scale,
        "mp",
        scatter_dimension=0,
        tiled=True,
    )


def gather_units(values):
    return lax.all_gather(values, "mp", axis=0, tiled=True)


def activate(sums, unit_count):
    gate_sum = sums[:, :unit_count]
    up_sum = sums[:, unit_count:]
    sigmoid_gate = jax.nn.sigmoid(gate_sum)
    return (gate_sum, up_sum, sigmoid_gate, gate_sum * sigmoid_gate)


def unit_grads(back_units, gate_sum, up_sum, sigmoid_gate, active):
    grad_gate = back_units * up_sum * sigmoid_gate * (1.0 + gate_sum * (1.0 - sigmoid_gate))
    grad_up = back_units * active
    return jnp.concatenate([grad_gate, grad_up], axis=1).astype(jnp.bfloat16)


def body(forget_rows, cotangent, retain_rows, w_gate, w_up, w_down):
    unit_count = w_gate.shape[1]
    width_scale = 1.0 / math.sqrt(D)
    contract_rows = (((0,), (0,)), ((), ()))
    contract_cols = (((1,), (1,)), ((), ()))
    forget_all, cotan_all, retain_all = (
        lax.all_gather(forget_rows, "dp", axis=0, tiled=True),
        lax.all_gather(cotangent, "dp", axis=0, tiled=True),
        lax.all_gather(retain_rows, "dp", axis=0, tiled=True),
    )
    total_rows = forget_all.shape[0]
    token_scale = 1.0 / math.sqrt(total_rows)
    weight_pair = jnp.concatenate([w_gate, w_up], axis=1)
    sums = project_sum(forget_all, weight_pair)
    gate_sum, up_sum, sigmoid_gate, active = activate(sums, unit_count)
    hidden = (active * up_sum).astype(jnp.bfloat16)
    hidden_all = gather_units(hidden)
    block_rows = cotan_all
    back_units = lax.psum_scatter(
        lax.dot_general(block_rows, w_down, contract_cols, preferred_element_type=jnp.float32)
        * width_scale,
        "mp",
        scatter_dimension=0,
        tiled=True,
    )
    grads_all = gather_units(unit_grads(back_units, gate_sum, up_sum, sigmoid_gate, active))
    grad_down = (
        lax.dot_general(hidden_all, cotan_all, contract_rows, preferred_element_type=jnp.float32)
        * token_scale
    )
    grad_pair = (
        lax.dot_general(forget_all, grads_all, contract_rows, preferred_element_type=jnp.float32)
        * token_scale
    )
    new_gate = (w_gate.astype(jnp.float32) + STEP_SIZE * grad_pair[:, :unit_count]).astype(
        jnp.bfloat16
    )
    new_up = (w_up.astype(jnp.float32) + STEP_SIZE * grad_pair[:, unit_count:]).astype(jnp.bfloat16)
    new_down = (w_down.astype(jnp.float32) + STEP_SIZE * grad_down).astype(jnp.bfloat16)
    new_pair = jnp.concatenate([new_gate, new_up], axis=1)
    keep_sums = project_sum(retain_all, new_pair)
    gate_keep, up_keep, sigmoid_keep, active_keep = activate(keep_sums, unit_count)
    hidden_keep = (active_keep * up_keep).astype(jnp.bfloat16)
    hidden_keep_all = gather_units(hidden_keep)
    out_scale = 1.0 / math.sqrt(FF)
    block_rows = hidden_keep_all
    retained = lax.psum_scatter(
        jnp.dot(block_rows, new_down, preferred_element_type=jnp.float32) * out_scale,
        "dp",
        scatter_dimension=0,
        tiled=True,
    ).astype(jnp.bfloat16)
    return (retained, new_gate, new_up, new_down)


def solution(mesh):
    in_specs = (
        P("dp", "mp"),
        P("dp", "mp"),
        P("dp", "mp"),
        P("mp", "dp"),
        P("mp", "dp"),
        P("dp", "mp"),
    )
    out_specs = (P("dp", "mp"), P("mp", "dp"), P("mp", "dp"), P("dp", "mp"))
    return jax.shard_map(body, mesh=mesh, in_specs=in_specs, out_specs=out_specs, check_vma=False)
```

profile of v0, /device:TPU:32, one launch (start us, length us, event | category | flops | bytes accessed | tf_op | source)
XLA Modules:
  0.0 805.6 jit_solution(11040523839631220439)
XLA Ops:
  7.2 0.7 all-gather.7.cloned.1.call-update
  7.9 0.7 all-gather.9.cloned.1.call-update
  8.7 96.4 %all-gather.7.cloned.1.call-done = bf16[1024,1024]{1,0:T(8,128)(2,1)} async-done(((bf16[32,1024]{1,0:T(8,128)(2,1)}), bf16[1024,1024]{1,0:T(8,128)(2,1)}) %all-gather.7.cloned.1.call-update) | async-done | bytes 2097168 | tf_op jit(solution)/shard_map/all_gather | solution.py:46
  105.1 4.5 convolution_multiply_fusion.1
  109.7 0.0 reduce-scatter.7.cloned.1.call-start
  109.7 84.6 %all-gather.9.cloned.1.call-done = bf16[1024,1024]{1,0:T(8,128)(2,1)} async-done(((bf16[32,1024]{1,0:T(8,128)(2,1)}), bf16[1024,1024]{1,0:T(8,128)(2,1)}) %all-gather.9.cloned.1.call-update) | async-done | bytes 2097168 | tf_op jit(solution)/shard_map/all_gather | solution.py:45
  194.3 5.9 multiply_bitcast_fusion.2
  200.2 0.0 all-gather.11.cloned.1.call-start
  200.2 28.7 %reduce-scatter.5.cloned.1.call-done = f32[128,512]{1,0:T(8,128)} async-done(((f32[1024,512]{1,0:T(8,128)}), f32[128,512]{1,0:T(8,128)}) %reduce-scatter.5.cloned.1.call-update) | async-done | bytes 262160 | tf_op jit(solution)/shard_map/reduce_scatter | solution.py:57
  229.0 56.2 %reduce-scatter.7.cloned.1.call-done = f32[128,1024]{1,0:T(8,128)} async-done(((f32[1024,1024]{1,0:T(8,128)}), f32[128,1024]{1,0:T(8,128)}) %reduce-scatter.7.cloned.1.call-update) | async-done | bytes 524304 | tf_op jit(solution)/shard_map/reduce_scatter | solution.py:14
  285.1 1.9 multiply_convert_fusion.2
  287.1 0.7 pad_maximum_fusion
  287.9 0.5 all-gather.13.cloned.1.call-update
  288.4 0.5 copy.10
  289.0 1.3 copy.12
  290.3 37.1 %all-gather.11.cloned.1.call-done = bf16[1024,1024]{1,0:T(8,128)(2,1)} async-done(((bf16[128,1024]{1,0:T(8,128)(2,1)}), bf16[1024,1024]{1,0:T(8,128)(2,1)}) %all-gather.11.cloned.1.call-update) | async-done | bytes 2097168 | tf_op jit(solution)/shard_map/all_gather | solution.py:23
  327.4 4.7 multiply_bitcast_fusion.1
  332.1 0.8 fusion.3
  332.9 91.1 %all-gather.13.cloned.1.call-done = bf16[1024,1024]{1,0:T(8,128)(2,1)} async-done(((bf16[32,1024]{1,0:T(8,128)(2,1)}), bf16[1024,1024]{1,0:T(8,128)(2,1)}) %all-gather.13.cloned.1.call-update) | async-done | bytes 2097168 | tf_op jit(solution)/shard_map/all_gather | solution.py:47
  424.0 5.9 multiply_bitcast_fusion
  430.0 0.7 all-gather.17.cloned.1.call-update
  430.7 45.1 %reduce-scatter.9.cloned.1.call-done = f32[128,1024]{1,0:T(8,128)} async-done(((f32[1024,1024]{1,0:T(8,128)}), f32[128,1024]{1,0:T(8,128)}) %reduce-scatter.9.cloned.1.call-update) | async-done | bytes 524304 | tf_op jit(solution)/shard_map/reduce_scatter | solution.py:14
  475.8 1.8 fusion.10
  477.6 0.0 reduce-scatter.11.cloned.1.call-start
  477.6 37.8 %all-gather.17.cloned.1.call-done = bf16[1024,512]{1,0:T(8,128)(2,1)} async-done(((bf16[128,512]{1,0:T(8,128)(2,1)}), bf16[1024,512]{1,0:T(8,128)(2,1)}) %all-gather.17.cloned.1.call-update) | async-done | bytes 1048592 | tf_op jit(solution)/shard_map/all_gather | solution.py:23
  515.4 4.2 add_convert_fusion
  519.5 34.3 %all-gather.15.cloned.1.call-done = bf16[1024,512]{1,0:T(8,128)(2,1)} async-done(((bf16[128,512]{1,0:T(8,128)(2,1)}), bf16[1024,512]{1,0:T(8,128)(2,1)}) %all-gather.15.cloned.1.call-update) | async-done | bytes 1048592 | tf_op jit(solution)/shard_map/all_gather | solution.py:23
  553.8 4.7 convolution_multiply_fusion
  558.6 1.3 copy.14
  559.9 1.3 copy.15
  561.2 236.0 %reduce-scatter.11.cloned.1.call-done = f32[32,1024]{1,0:T(8,128)} async-done(((f32[1024,1024]{1,0:T(8,128)}), f32[32,1024]{1,0:T(8,128)}) %reduce-scatter.11.cloned.1.call-update) | async-done | bytes 131088 | tf_op jit(solution)/shard_map/reduce_scatter | solution.py:85
  797.2 1.5 convert_element_type.36
  (21 shorter events, 0.4 us)
Async XLA Ops:
  7.2 97.9 %all-gather.7.cloned.1.call-start = ((), (), s32[]{:S(2)}) async-start(), calls=%async_computation.4 | async-start | bytes 2162688 | tf_op jit(solution)/shard_map/all_gather | solution.py:46
  7.9 186.4 %all-gather.9.cloned.1.call-start = ((), (), s32[]{:S(2)}) async-start(), calls=%async_computation.6 | async-start | bytes 2162688 | tf_op jit(solution)/shard_map/all_gather | solution.py:45
  8.6 220.3 %reduce-scatter.5.cloned.1.call-start = ((), (), s32[]{:S(2)}) async-start(), calls=%async_computation.5 | async-start | bytes 2359296 | tf_op jit(solution)/shard_map/reduce_scatter | solution.py:57
  109.6 84.7 %copy-start.1 = (bf16[1024,512]{1,0:T(8,128)(2,1)S(1)}, bf16[1024,512]{1,0:T(8,128)(2,1)}, u32[]{:S(2)}) copy-start(bf16[1024,512]{1,0:T(8,128)(2,1)} %param.9) | copy-start | bytes 3145732
  109.6 84.7 %copy-start.2 = (bf16[1024,512]{1,0:T(8,128)(2,1)S(1)}, bf16[1024,512]{1,0:T(8,128)(2,1)}, u32[]{:S(2)}) copy-start(bf16[1024,512]{1,0:T(8,128)(2,1)} %param.10) | copy-start | bytes 3145732
  109.7 175.5 %reduce-scatter.7.cloned.1.call-start = ((), (), s32[]{:S(2)}) async-start(), calls=%async_computation.7 | async-start | bytes 4718592 | tf_op jit(solution)/shard_map/reduce_scatter | solution.py:14
  200.2 127.2 %all-gather.11.cloned.1.call-start = ((), (), s32[]{:S(2)}) async-start(), calls=%async_computation.8 | async-start | bytes 2359296 | tf_op jit(solution)/shard_map/all_gather | solution.py:23
  287.8 136.2 %all-gather.13.cloned.1.call-start = ((), (), s32[]{:S(2)}) async-start(), calls=%async_computation.9 | async-start | bytes 2162688 | tf_op jit(solution)/shard_map/all_gather | solution.py:47
  288.4 187.4 %reduce-scatter.9.cloned.1.call-start = ((), (), s32[]{:S(2)}) async-start(), calls=%async_computation.10 | async-start | bytes 4718592 | tf_op jit(solution)/shard_map/reduce_scatter | solution.py:14
  327.4 4.7 copy-start
  429.9 85.5 %copy-start.3 = (bf16[512,1024]{1,0:T(8,128)(2,1)S(1)}, bf16[512,1024]{1,0:T(8,128)(2,1)}, u32[]{:S(2)}) copy-start(bf16[512,1024]{1,0:T(8,128)(2,1)} %param.11) | copy-start | bytes 3145732
  429.9 85.5 %all-gather.17.cloned.1.call-start = ((), (), s32[]{:S(2)}) async-start(), calls=%async_computation.12 | async-start | bytes 1179648 | tf_op jit(solution)/shard_map/all_gather | solution.py:23
  430.7 123.1 %all-gather.15.cloned.1.call-start = ((), (), s32[]{:S(2)}) async-start(), calls=%async_computation.11 | async-start | bytes 1179648 | tf_op jit(solution)/shard_map/all_gather | solution.py:23
  477.6 319.6 %reduce-scatter.11.cloned.1.call-start = ((), (), s32[]{:S(2)}) async-start(), calls=%async_computation.13 | async-start | bytes 4325376 | tf_op jit(solution)/shard_map/reduce_scatter | solution.py:85
Sparse Core Ops, SparseCore 0:
  11.5 93.5 all-gather.6
  108.6 85.6 all-gather.8
  196.8 32.0 reduce-scatter.4
  231.4 53.7 reduce-scatter.6
  287.9 39.4 all-gather.10
  330.8 93.1 all-gather.12
  430.0 45.6 reduce-scatter.8
  478.1 37.1 all-gather.16
  517.7 36.0 all-gather.14
  558.7 238.4 reduce-scatter.10
where the time goes:
time: 806 us
  waiting for transfers between devices  750 us (93%)
  matrix products  29.9 us (4%)
  between operations  14.2 us (2%)
    reduce_scatter x1, waiting for transfers between devices, body(): lax.psum_scatter(jnp.dot(block_rows, new_down, preferred_element_type=jnp...  236 us
    all_gather x3, waiting for transfers between devices, gather_units(): return lax.all_gather(values, 'mp', axis=0, tiled=True)  109 us
    reduce_scatter x2, waiting for transfers between devices, project_sum(): lax.psum_scatter(jnp.dot(rows_all, weight_pair, preferred_element_type=jn...  101 us
    all_gather x1, waiting for transfers between devices, body(): lax.all_gather(cotangent, 'dp', axis=0, tiled=True)  96.4 us
    all_gather x1, waiting for transfers between devices, body(): lax.all_gather(retain_rows, 'dp', axis=0, tiled=True)  91.1 us
    all_gather x1, waiting for transfers between devices, body(): lax.all_gather(forget_rows, 'dp', axis=0, tiled=True)  84.6 us
    reduce_scatter x1, waiting for transfers between devices, body(): lax.psum_scatter(lax.dot_general(block_rows, w_down, contract_cols, prefe...  28.7 us
  transfers between devices with their start and end apart: 10, of which 10 were waited for; matrix products, arithmetic and copies ran while one was open for 3% of the time, Pallas kernels for 0%

commit v1 on v0

--- a/solution.py
+++ b/solution.py
@@ -43,7 +43,9 @@
     contract_cols = (((1,), (1,)), ((), ()))
     forget_all, cotan_all, retain_all = (
         lax.all_gather(forget_rows, "dp", axis=0, tiled=True),
-        lax.all_gather(cotangent, "dp", axis=0, tiled=True),
+        jnp.concatenate(
+            lax.all_to_all(jnp.stack([cotangent] * lax.axis_size("dp")), "dp", 0, 0), axis=0
+        ),
         lax.all_gather(retain_rows, "dp", axis=0, tiled=True),
     )
     total_rows = forget_all.shape[0]

time: 806 us -> 708 us (0.88)
  waiting for transfers between devices: 750 us -> 636 us
  starting transfers between devices: 0.4 us -> 13.7 us
    all_gather x1 -> x0, waiting for transfers between devices: 96.4 us -> none  [body(): lax.all_gather(cotangent, 'dp', axis=0, tiled=True)]
    all_to_all x0 -> x1, waiting for transfers between devices: none -> 55.9 us  [body(): lax.all_to_all(jnp.stack([cotangent] * lax.axis_size('dp')), 'dp', 0, 0)]
    all_gather x1, waiting for transfers between devices: 84.6 us -> 47 us  [body(): lax.all_gather(forget_rows, 'dp', axis=0, tiled=True)]
    reduce_scatter x1, waiting for transfers between devices: 28.7 us -> 0.02 us  [body(): lax.psum_scatter(lax.dot_general(block_rows, w_down, contract_cols, prefe...]
    all_to_all x0 -> x1, starting transfers between devices: none -> 13.2 us  [body(): lax.all_to_all(jnp.stack([cotangent] * lax.axis_size('dp')), 'dp', 0, 0)]
  transfers between devices with their start and end apart: 10 -> 10, of which waited for: 10 -> 9; matrix products, arithmetic and copies ran while one was open for 3% -> 3% of each run, Pallas kernels for 0% -> 0%
where the time goes in v1:
time: 708 us; the launch traced here: 707 us
  waiting for transfers between devices  636 us (90%)
  matrix products  28 us (4%)
  between operations  15.6 us (2%)
  starting transfers between devices  13.7 us (2%)
    reduce_scatter x1, waiting for transfers between devices, body(): lax.psum_scatter(jnp.dot(block_rows, new_down, preferred_element_type=jnp...  235 us
    all_gather x3, waiting for transfers between devices, gather_units(): return lax.all_gather(values, 'mp', axis=0, tiled=True)  108 us
    reduce_scatter x2, waiting for transfers between devices, project_sum(): lax.psum_scatter(jnp.dot(rows_all, weight_pair, preferred_element_type=jn...  96.1 us
    all_gather x1, waiting for transfers between devices, body(): lax.all_gather(retain_rows, 'dp', axis=0, tiled=True)  91.6 us
    all_to_all x1, waiting for transfers between devices, body(): lax.all_to_all(jnp.stack([cotangent] * lax.axis_size('dp')), 'dp', 0, 0)  55.9 us
    all_gather x1, waiting for transfers between devices, body(): lax.all_gather(forget_rows, 'dp', axis=0, tiled=True)  47 us
  transfers between devices with their start and end apart: 10, of which 9 were waited for; matrix products, arithmetic and copies ran while one was open for 3% of the time, Pallas kernels for 0%

profile of v1, /device:TPU:32, one launch (start us, length us, event | category | flops | bytes accessed | tf_op | source)
XLA Modules:
  0.0 707.1 jit_solution(4626845556636008805)
XLA Ops:
  8.0 2.4 stack.2
  10.4 13.2 %all-to-all-start = ((bf16[32,32,1024]{2,1,0:T(8,128)(2,1)}), bf16[32,32,1024]{2,1,0:T(8,128)(2,1)S(1)}, u32[]{:S(2)}, u32[]{:S(2)}) async-start(bf16[32,32,1024]{2,1,0:T(8,128)(2,1)} %stack.2), calls=%async_computation | async-start | bytes 4194304 | tf_op jit(solution)/shard_map/all_to_all | solution.py:47
  23.7 0.7 all-gather.6.cloned.1.call-update
  24.4 55.9 %all-to-all-done = bf16[32,32,1024]{2,1,0:T(8,128)(2,1)S(1)} async-done(((bf16[32,32,1024]{2,1,0:T(8,128)(2,1)}), bf16[32,32,1024]{2,1,0:T(8,128)(2,1)S(1)}, u32[]{:S(2)}, u32[]{:S(2)}) %all-to-all-start) | async-done | bytes 2097184 | tf_op jit(solution)/shard_map/all_to_all | solution.py:47
  80.3 2.7 convolution_multiply_fusion.1
  83.1 0.0 reduce-scatter.7.cloned.1.call-start
  83.1 47.0 %all-gather.6.cloned.1.call-done = bf16[1024,1024]{1,0:T(8,128)(2,1)} async-done(((bf16[32,1024]{1,0:T(8,128)(2,1)}), bf16[1024,1024]{1,0:T(8,128)(2,1)}) %all-gather.6.cloned.1.call-update) | async-done | bytes 2097168 | tf_op jit(solution)/shard_map/all_gather | solution.py:45
  130.1 5.9 multiply_bitcast_fusion.2
  136.0 0.0 all-gather.8.cloned.1.call-start
  136.1 51.0 %reduce-scatter.7.cloned.1.call-done = f32[128,1024]{1,0:T(8,128)} async-done(((f32[1024,1024]{1,0:T(8,128)}), f32[128,1024]{1,0:T(8,128)}) %reduce-scatter.7.cloned.1.call-update) | async-done | bytes 524304 | tf_op jit(solution)/shard_map/reduce_scatter | solution.py:14
  187.1 1.9 multiply_convert_fusion.2
  189.0 0.7 pad_maximum_fusion
  189.8 0.7 all-gather.10.cloned.1.call-update
  190.6 0.5 copy.10
  191.1 1.3 copy.12
  192.4 36.6 %all-gather.8.cloned.1.call-done = bf16[1024,1024]{1,0:T(8,128)(2,1)} async-done(((bf16[128,1024]{1,0:T(8,128)(2,1)}), bf16[1024,1024]{1,0:T(8,128)(2,1)}) %all-gather.8.cloned.1.call-update) | async-done | bytes 2097168 | tf_op jit(solution)/shard_map/all_gather | solution.py:23
  229.0 4.7 multiply_bitcast_fusion.1
  233.8 0.8 fusion.3
  234.5 91.6 %all-gather.10.cloned.1.call-done = bf16[1024,1024]{1,0:T(8,128)(2,1)} async-done(((bf16[32,1024]{1,0:T(8,128)(2,1)}), bf16[1024,1024]{1,0:T(8,128)(2,1)}) %all-gather.10.cloned.1.call-update) | async-done | bytes 2097168 | tf_op jit(solution)/shard_map/all_gather | solution.py:49
  326.1 5.9 multiply_bitcast_fusion
  332.1 0.7 all-gather.14.cloned.1.call-update
  332.8 45.1 %reduce-scatter.9.cloned.1.call-done = f32[128,1024]{1,0:T(8,128)} async-done(((f32[1024,1024]{1,0:T(8,128)}), f32[128,1024]{1,0:T(8,128)}) %reduce-scatter.9.cloned.1.call-update) | async-done | bytes 524304 | tf_op jit(solution)/shard_map/reduce_scatter | solution.py:14
  377.9 1.8 fusion.10
  379.7 0.2 reduce-scatter.11.cloned.1.call-start
  379.9 37.4 %all-gather.14.cloned.1.call-done = bf16[1024,512]{1,0:T(8,128)(2,1)} async-done(((bf16[128,512]{1,0:T(8,128)(2,1)}), bf16[1024,512]{1,0:T(8,128)(2,1)}) %all-gather.14.cloned.1.call-update) | async-done | bytes 1048592 | tf_op jit(solution)/shard_map/all_gather | solution.py:23
  417.3 4.2 add_convert_fusion
  421.4 34.1 %all-gather.12.cloned.1.call-done = bf16[1024,512]{1,0:T(8,128)(2,1)} async-done(((bf16[128,512]{1,0:T(8,128)(2,1)}), bf16[1024,512]{1,0:T(8,128)(2,1)}) %all-gather.12.cloned.1.call-update) | async-done | bytes 1048592 | tf_op jit(solution)/shard_map/all_gather | solution.py:23
  455.5 4.7 convolution_multiply_fusion
  460.2 1.3 copy.14
  461.6 1.3 copy.15
  462.9 235.3 %reduce-scatter.11.cloned.1.call-done = f32[32,1024]{1,0:T(8,128)} async-done(((f32[1024,1024]{1,0:T(8,128)}), f32[32,1024]{1,0:T(8,128)}) %reduce-scatter.11.cloned.1.call-update) | async-done | bytes 131088 | tf_op jit(solution)/shard_map/reduce_scatter | solution.py:87
  698.1 1.5 convert_element_type.36
  (27 shorter events, 0.4 us)
Async XLA Ops:
  10.4 69.9 %copy-start.5 = (bf16[512,1024]{1,0:T(8,128)(2,1)S(1)}, bf16[512,1024]{1,0:T(8,128)(2,1)}, u32[]{:S(2)}) copy-start(bf16[512,1024]{1,0:T(8,128)(2,1)} %param.11) | copy-start | bytes 3145732
  10.4 69.9 %all-to-all-start = ((bf16[32,32,1024]{2,1,0:T(8,128)(2,1)}), bf16[32,32,1024]{2,1,0:T(8,128)(2,1)S(1)}, u32[]{:S(2)}, u32[]{:S(2)}) async-start(bf16[32,32,1024]{2,1,0:T(8,128)(2,1)} %stack.2), calls=%async_computation | async-start | bytes 4194304 | tf_op jit(solution)/shard_map/all_to_all | solution.py:47
  23.6 106.5 %all-gather.6.cloned.1.call-start = ((), (), s32[]{:S(2)}) async-start(), calls=%async_computation.6 | async-start | bytes 2162688 | tf_op jit(solution)/shard_map/all_gather | solution.py:45
  24.4 111.7 %reduce-scatter.5.cloned.1.call-start = ((), (), s32[]{:S(2)}) async-start(), calls=%async_computation.5 | async-start | bytes 2359296 | tf_op jit(solution)/shard_map/reduce_scatter | solution.py:59
  80.3 2.7 copy-start.1
  83.0 47.1 %copy-start.2 = (bf16[1024,512]{1,0:T(8,128)(2,1)S(1)}, bf16[1024,512]{1,0:T(8,128)(2,1)}, u32[]{:S(2)}) copy-start(bf16[1024,512]{1,0:T(8,128)(2,1)} %param.9) | copy-start | bytes 3145732
  83.0 47.1 %copy-start.4 = (bf16[1024,512]{1,0:T(8,128)(2,1)S(1)}, bf16[1024,512]{1,0:T(8,128)(2,1)}, u32[]{:S(2)}) copy-start(bf16[1024,512]{1,0:T(8,128)(2,1)} %param.10) | copy-start | bytes 3145732
  83.1 104.0 %reduce-scatter.7.cloned.1.call-start = ((), (), s32[]{:S(2)}) async-start(), calls=%async_computation.7 | async-start | bytes 4718592 | tf_op jit(solution)/shard_map/reduce_scatter | solution.py:14
  136.0 54.6 %copy-start.3 = (bf16[1024,512]{1,0:T(8,128)(2,1)S(1)}, bf16[1024,512]{1,0:T(8,128)(2,1)}, u32[]{:S(2)}) copy-start(bf16[1024,512]{1,0:T(8,128)(2,1)} %param.9) | copy-start | bytes 3145732
  136.0 93.0 %all-gather.8.cloned.1.call-start = ((), (), s32[]{:S(2)}) async-start(), calls=%async_computation.8 | async-start | bytes 2359296 | tf_op jit(solution)/shard_map/all_gather | solution.py:23
  189.8 136.3 %all-gather.10.cloned.1.call-start = ((), (), s32[]{:S(2)}) async-start(), calls=%async_computation.9 | async-start | bytes 2162688 | tf_op jit(solution)/shard_map/all_gather | solution.py:49
  190.5 187.4 %reduce-scatter.9.cloned.1.call-start = ((), (), s32[]{:S(2)}) async-start(), calls=%async_computation.10 | async-start | bytes 4718592 | tf_op jit(solution)/shard_map/reduce_scatter | solution.py:14
  229.0 4.7 copy-start
  332.0 85.3 %copy-start.6 = (bf16[512,1024]{1,0:T(8,128)(2,1)S(1)}, bf16[512,1024]{1,0:T(8,128)(2,1)}, u32[]{:S(2)}) copy-start(bf16[512,1024]{1,0:T(8,128)(2,1)} %param.11) | copy-start | bytes 3145732
  332.0 85.2 %all-gather.14.cloned.1.call-start = ((), (), s32[]{:S(2)}) async-start(), calls=%async_computation.12 | async-start | bytes 1179648 | tf_op jit(solution)/shard_map/all_gather | solution.py:23
  332.8 122.7 %all-gather.12.cloned.1.call-start = ((), (), s32[]{:S(2)}) async-start(), calls=%async_computation.11 | async-start | bytes 1179648 | tf_op jit(solution)/shard_map/all_gather | solution.py:23
  379.7 318.5 %reduce-scatter.11.cloned.1.call-start = ((), (), s32[]{:S(2)}) async-start(), calls=%async_computation.13 | async-start | bytes 4325376 | tf_op jit(solution)/shard_map/reduce_scatter | solution.py:87
Sparse Core Ops, SparseCore 0:
  28.0 102.1 all-gather.5
  460.4 237.7 reduce-scatter.10
Sparse Core Ops, SparseCore 1:
  83.1 45.4 reduce-scatter.4
  136.1 50.9 reduce-scatter.6
  189.9 39.1 all-gather.7
  232.6 93.4 all-gather.9
  332.1 45.7 reduce-scatter.8
  380.3 36.9 all-gather.13
  419.5 35.9 all-gather.11
